TPU v7x, 256 devices: a whole 4x4x8 slice. The times are simulated.
256 devices in a mesh: dp: 32 (over x, y, core), expert: 8 (over z).
Axes of the slice: x: 4, y: 4, z: 8, core: 2. Of those that a mesh axis runs over, the one named last changes fastest.
Arguments:
- tokens: bfloat16 [32768, 2048], P(('dp', 'expert')), may hold values from -6 to 6
- expert_ids: int32 [32768, 3], P(('dp', 'expert')), may hold values from 0 to 7, as said below
- slot_index: int32 [32768, 3], P(('dp', 'expert')), may hold values from -1 to 47, as said below
- w_router: float32 [2048, 8], replicated, may hold values from -0.125 to 0.125
- w_gate: bfloat16 [8, 2048, 768], P('expert'), may hold values from -0.125 to 0.125
- w_up: bfloat16 [8, 2048, 768], P('expert'), may hold values from -0.125 to 0.125
- w_down: bfloat16 [8, 2048, 768], P('expert'), may hold values from -0.21875 to 0.21875
- grad_out: bfloat16 [32768, 2048], P(('dp', 'expert')), may hold values from -0.59765625 to 0.59765625
Outputs:
- layer_output: bfloat16 [32768, 2048], P(('dp', 'expert'))
- grad_tokens: bfloat16 [32768, 2048], P(('dp', 'expert'))
- grad_router: float32 [2048, 8], replicated
- grad_gate: float32 [8, 2048, 768], P('expert', 'dp')
- grad_up: float32 [8, 2048, 768], P('expert', 'dp')
- grad_down: float32 [8, 2048, 768], P('expert', 'dp')
Inputs may be any that keep to these rules, and one draw needn't show every extreme that they name: `expert_ids`: each token names 3 different experts. `slot_index`: the live choices of one device's 128 tokens to one expert take the slots 0, 1, 2, ... in the order of tokens and then choices, and choices past 48 of them get -1; in every draw some expert gets all 48 slots from every device.
All inputs are finite; a program needn't handle non-finite values.
Results may differ from a plain program's by a relative error of at most 0.025.
Values may be sent and summed in bfloat16 or wider, within the bound.
No kernel may reach another device: no remote copies, remote signals or barrier semaphores. Data moves between devices by JAX's collectives and lax.ppermute only.
A program may use at most 128 MiB of HBM per device.

v0:
```python
import jax
import jax.numpy as jnp
from jax import lax
from jax.sharding import PartitionSpec as P


def silu_parts(hidden):
    sigmoid_val = jax.nn.sigmoid(hidden)
    return (hidden * sigmoid_val, sigmoid_val * (1.0 + hidden * (1.0 - sigmoid_val)))


def on_device(tokens, expert_ids, slot_index, w_router, w_gate, w_up, w_down, grad_out):
    tok_count, width = tokens.shape
    choice_count = expert_ids.shape[1]
    expert_count = w_router.shape[1]
    local_count = w_gate.shape[0]
    hidden_width = w_gate.shape[2]
    sender_count = lax.axis_size("expert")
    own_rows = width // lax.axis_size("dp")
    slot_count = tok_count * choice_count // expert_count
    highest = lax.Precision.HIGHEST
    tokens_wide = tokens.astype(jnp.float32)
    scores = jax.nn.sigmoid(jnp.dot(tokens_wide, w_router, precision=highest))
    picker = (
        expert_ids[:, :, None] == jnp.arange(expert_count, dtype=jnp.int32)[None, None, :]
    ).astype(jnp.float32)
    picked = jnp.sum(picker * scores[:, None, :], axis=2)
    pick_sum = jnp.sum(picked, axis=1, keepdims=True)
    gate_value = picked / pick_sum
    is_live = slot_index >= 0
    live_gate = jnp.where(is_live, gate_value, 0.0)
    position = jnp.where(is_live, expert_ids * slot_count + slot_index, expert_count * slot_count)
    owner_table = jnp.full((expert_count * slot_count + 1,), tok_count * choice_count, jnp.int32)
    owner_table = owner_table.at[position.reshape(-1)].set(
        jnp.arange(tok_count * choice_count, dtype=jnp.int32)
    )
    owner_table = owner_table[: expert_count * slot_count]
    zero_row = jnp.zeros((1, width), jnp.bfloat16)
    token_pad = jnp.concatenate([tokens, zero_row], axis=0)
    outgoing = token_pad[owner_table // choice_count].reshape(expert_count, slot_count, width)
    received = lax.all_to_all(outgoing, "expert", split_axis=0, concat_axis=0, tiled=True)
    item_count = received.shape[1]
    expert_row_block = received.reshape(sender_count, local_count, item_count, width)
    hidden_gate = jnp.einsum(
        "slnd,ldf->slnf", expert_row_block, w_gate, preferred_element_type=jnp.float32
    )
    hidden_up = jnp.einsum(
        "slnd,ldf->slnf", expert_row_block, w_up, preferred_element_type=jnp.float32
    )
    expert_activated = (silu_parts(hidden_gate)[0] * hidden_up).astype(jnp.bfloat16)
    expert_out = jnp.einsum(
        "slnf,ldf->slnd", expert_activated, w_down, preferred_element_type=jnp.float32
    ).astype(jnp.bfloat16)
    returned = lax.all_to_all(
        expert_out.reshape(sender_count * local_count, item_count, width),
        "expert",
        split_axis=0,
        concat_axis=0,
        tiled=True,
    )
    flat_shape = (sender_count * local_count, item_count, hidden_width)
    results = (
        returned,
        received,
        hidden_gate.reshape(flat_shape),
        hidden_up.reshape(flat_shape),
        expert_activated.reshape(flat_shape),
    )
    returned = results[0]
    received = results[1]
    out_pad = jnp.concatenate([returned.reshape(-1, width), zero_row], axis=0)
    dy_wide = grad_out.astype(jnp.float32)
    mixed = jnp.zeros((tok_count, width), jnp.float32)
    gate_grads = []
    for which in range(choice_count):
        got_row = out_pad[position[:, which]].astype(jnp.float32)
        mixed = mixed + live_gate[:, which : which + 1] * got_row
        gate_grads.append(jnp.sum(dy_wide * got_row, axis=1))
    layer_output = mixed.astype(jnp.bfloat16)
    gate_grad = jnp.stack(gate_grads, axis=1)
    gate_pad = jnp.concatenate([live_gate.reshape(-1), jnp.zeros((1,), jnp.float32)])
    grad_pad = jnp.concatenate([grad_out, zero_row], axis=0)
    grad_rows = (
        gate_pad[owner_table][:, None] * grad_pad[owner_table // choice_count].astype(jnp.float32)
    ).astype(jnp.bfloat16)
    grad_rows = grad_rows.reshape(expert_count, slot_count, width)
    block_shape = (sender_count, local_count, slot_count, width)
    arrived = lax.all_to_all(grad_rows, "expert", split_axis=0, concat_axis=0, tiled=True).reshape(
        block_shape
    )
    row_block = received.reshape(block_shape)
    hidden_shape = (sender_count, local_count, slot_count, hidden_width)
    hidden_gate = results[2].reshape(hidden_shape)
    hidden_up = results[3].reshape(hidden_shape)
    activated = results[4].reshape(hidden_shape)
    silu_value, silu_slope = silu_parts(hidden_gate)
    grad_act = jnp.einsum("slnd,ldf->slnf", arrived, w_down, preferred_element_type=jnp.float32)
    gate_delta = (grad_act * hidden_up * silu_slope).astype(jnp.bfloat16)
    up_delta = (grad_act * silu_value).astype(jnp.bfloat16)
    row_grad = (
        jnp.einsum("slnf,ldf->slnd", gate_delta, w_gate, preferred_element_type=jnp.float32)
        + jnp.einsum("slnf,ldf->slnd", up_delta, w_up, preferred_element_type=jnp.float32)
    ).astype(jnp.bfloat16)
    sent_back = lax.all_to_all(
        row_grad.reshape(sender_count * local_count, slot_count, width),
        "expert",
        split_axis=0,
        concat_axis=0,
        tiled=True,
    )
    piece = row_block
    gate_part = jnp.einsum("slnd,slnf->dlf", piece, gate_delta, preferred_element_type=jnp.float32)
    up_part = jnp.einsum("slnd,slnf->dlf", piece, up_delta, preferred_element_type=jnp.float32)
    gate_part, up_part = (gate_part, up_part)
    piece = arrived
    down_part = (
        jnp.einsum("slnd,slnf->dlf", piece, activated, preferred_element_type=jnp.float32)
        .reshape(lax.axis_size("dp") * own_rows, local_count * hidden_width)
        .reshape(lax.axis_size("dp") * own_rows, local_count, hidden_width)
    )
    joined = lax.psum_scatter(
        jnp.concatenate([gate_part, up_part, down_part], axis=2)
        .reshape(lax.axis_size("dp") * own_rows, local_count * 3 * hidden_width)
        .astype(jnp.bfloat16),
        "dp",
        scatter_dimension=0,
        tiled=True,
    ).astype(jnp.float32)
    triple_view = joined.reshape(-1, local_count, 3, hidden_width)
    grad_gate = jnp.transpose(triple_view[:, :, 0, :], (1, 0, 2))
    grad_up = jnp.transpose(triple_view[:, :, 1, :], (1, 0, 2))
    grad_down = jnp.transpose(triple_view[:, :, 2, :], (1, 0, 2))
    back_pad = jnp.concatenate([sent_back.reshape(-1, width), zero_row], axis=0)
    row_sum = jnp.zeros((tok_count, width), jnp.float32)
    for which in range(choice_count):
        row_sum = row_sum + back_pad[position[:, which]].astype(jnp.float32)
    cross_term = jnp.sum(gate_grad * gate_value, axis=1, keepdims=True)
    pick_delta = (gate_grad - cross_term) / pick_sum * picked * (1.0 - picked)
    logit_grad = jnp.sum(picker * pick_delta[:, :, None], axis=1)
    grad_tokens = (row_sum + jnp.dot(logit_grad, w_router.T, precision=highest)).astype(
        jnp.bfloat16
    )
    grad_router = lax.psum(jnp.dot(tokens_wide.T, logit_grad, precision=highest), ("dp", "expert"))
    return (layer_output, grad_tokens, grad_router, grad_gate, grad_up, grad_down)


def solution(mesh):
    return jax.shard_map(
        on_device,
        mesh=mesh,
        in_specs=(
            P(("dp", "expert"), None),
            P(("dp", "expert"), None),
            P(("dp", "expert"), None),
            P(),
            P("expert", None, None),
            P("expert", None, None),
            P("expert", None, None),
            P(("dp", "expert"), None),
        ),
        out_specs=(
            P(("dp", "expert"), None),
            P(("dp", "expert"), None),
            P(),
            P("expert", "dp", None),
            P("expert", "dp", None),
            P("expert", "dp", None),
        ),
        check_vma=False,
    )
```

profile of v0, /device:TPU:1, one launch (start us, length us, event | category | flops | bytes accessed | tf_op | source)
XLA Modules:
  0.0 503.2 jit_solution(17069465970971020080)
XLA Ops:
  8.0 0.0 copy-start
  8.0 0.9 add_select_fusion.1
  8.9 0.1 copy.36
  9.0 0.2 reshape.191
  9.2 2.9 scatter_custom_fusion
  12.2 1.9 concatenate.23
  14.1 6.2 %gather_fusion = bf16[384,2048]{1,0:T(8,128)(2,1)} fusion(bf16[129,2048]{1,0:T(8,128)(2,1)} %concatenate.23, s32[1024]{0:T(1024)S(1)} %get-tuple-element.27), kind=kCustom, calls=%fused_computation | custom fusion | bytes 3147264 | tf_op jit(solution)/shard_map/gather | solution.py:40
  20.3 9.0 %all-to-all-start = ((bf16[8,48,2048]{2,1,0:T(8,128)(2,1)}), bf16[8,48,2048]{2,1,0:T(8,128)(2,1)}, u32[]{:S(2)}, u32[]{:S(2)}) async-start(bf16[8,48,2048]{2,1,0:T(8,128)(2,1)} %bitcast.129), calls=%async_computation | async-start | bytes 3145728 | tf_op jit(solution)/shard_map/all_to_all | solution.py:41
  29.3 1.9 concatenate.26
  31.2 6.2 %gather_fusion.5 = bf16[384,2048]{1,0:T(8,128)(2,1)} fusion(bf16[129,2048]{1,0:T(8,128)(2,1)} %concatenate.26, s32[1024]{0:T(1024)S(1)} %get-tuple-element.27), kind=kCustom, calls=%fused_computation.5 | custom fusion | bytes 3147264 | tf_op jit(solution)/shard_map/gather | solution.py:84
  37.4 0.0 copy-done.2
  37.4 1.6 fusion.34
  38.9 0.0 copy-done.3
  39.0 0.0 copy-done.4
  39.0 0.1 copy.37
  39.1 0.2 reshape.198
  39.3 2.8 gather_fusion.4
  42.1 0.1 mul.126
  42.2 2.9 fusion
  45.1 24.7 %all-to-all-done = bf16[8,48,2048]{2,1,0:T(8,128)(2,1)} async-done(((bf16[8,48,2048]{2,1,0:T(8,128)(2,1)}), bf16[8,48,2048]{2,1,0:T(8,128)(2,1)}, u32[]{:S(2)}, u32[]{:S(2)}) %all-to-all-start) | async-done | bytes 1572896 | tf_op jit(solution)/shard_map/all_to_all | solution.py:41
  69.8 4.3 all-to-all-start.2
  74.1 0.2 reduce-scatter.4.cloned.1.call-start
  74.3 0.0 copy-start.5
  74.4 5.0 fusion.22
  79.3 0.0 copy-done.5
  79.3 3.8 fusion.25
  83.1 29.2 %all-to-all-done.2 = bf16[8,48,2048]{2,1,0:T(8,128)(2,1)} async-done(((bf16[8,48,2048]{2,1,0:T(8,128)(2,1)}), bf16[8,48,2048]{2,1,0:T(8,128)(2,1)}, u32[]{:S(2)}, u32[]{:S(2)}) %all-to-all-start.2) | async-done | bytes 1572896 | tf_op jit(solution)/shard_map/all_to_all | solution.py:88
  112.4 0.0 copy-done
  112.4 3.7 multiply_convert_fusion.1
  116.1 3.9 fusion.15
  120.0 3.3 fusion.14
  123.3 0.0 copy-done.7
  123.3 3.2 fusion.13
  126.6 4.5 maximum_bitcast_fusion
  131.0 12.4 %copy.41 = bf16[2048,2304]{1,0:T(8,128)(2,1)} copy(bf16[2048,2304]{0,1:T(8,128)(2,1)} %maximum_bitcast_fusion) | data formatting | bytes 18874368
  143.4 0.0 reduce-scatter.4.cloned.1.call-update
  143.4 3.7 fusion.18
  147.1 4.5 all-to-all-start.1
  151.6 0.0 copy-start.6
  151.7 3.8 fusion.5
  155.5 2.6 add_convert_fusion
  158.1 31.7 %all-to-all-done.1 = bf16[8,48,2048]{2,1,0:T(8,128)(2,1)} async-done(((bf16[8,48,2048]{2,1,0:T(8,128)(2,1)}), bf16[8,48,2048]{2,1,0:T(8,128)(2,1)}, u32[]{:S(2)}, u32[]{:S(2)}) %all-to-all-start.1) | async-done | bytes 1572896 | tf_op jit(solution)/shard_map/all_to_all | solution.py:54
  189.8 4.3 all-to-all-start.3
  194.1 0.0 all-reduce.6.cloned.1.call-start
  194.2 2.8 concatenate.24
  197.0 4.3 gather_fusion.2
  201.3 3.9 gather_fusion.3
  205.2 27.1 %all-to-all-done.3 = bf16[8,48,2048]{2,1,0:T(8,128)(2,1)} async-done(((bf16[8,48,2048]{2,1,0:T(8,128)(2,1)}), bf16[8,48,2048]{2,1,0:T(8,128)(2,1)}, u32[]{:S(2)}, u32[]{:S(2)}) %all-to-all-start.3) | async-done | bytes 1572896 | tf_op jit(solution)/shard_map/all_to_all | solution.py:104
  232.3 2.8 concatenate.27
  235.1 3.9 gather_fusion.8
  239.0 3.9 gather_fusion.7
  242.9 3.9 gather_fusion.1
  246.8 3.9 gather_fusion.6
  250.6 3.0 fusion.38
  253.7 1.0 convolution_bitcast_fusion
  254.7 0.0 all-reduce.6.cloned.1.call-update
  254.7 3.3 fusion.21
  258.0 2.0 copy.42
  260.0 2.1 fusion.53
  262.1 1.8 copy.43
  263.9 1.8 copy.44
  265.7 0.8 copy.45
  266.6 227.7 %all-reduce.6.cloned.1.call-done = f32[2048,8]{0,1:T(8,128)} async-done(((f32[2048,8]{0,1:T(8,128)}), f32[2048,8]{0,1:T(8,128)}) %all-reduce.6.cloned.1.call-update) | async-done | bytes 65552 | tf_op jit(solution)/shard_map/psum | solution.py:143
  494.3 1.5 copy.47
  (28 shorter events, 0.2 us)
Async XLA Ops:
  8.0 104.4 %copy-start = (bf16[1,2048,768]{2,1,0:T(8,128)(2,1)S(1)}, bf16[1,2048,768]{2,1,0:T(8,128)(2,1)}, u32[]{:S(2)}) copy-start(bf16[1,2048,768]{2,1,0:T(8,128)(2,1)} %param.14) | copy-start | bytes 9437188
  20.3 49.5 %all-to-all-start = ((bf16[8,48,2048]{2,1,0:T(8,128)(2,1)}), bf16[8,48,2048]{2,1,0:T(8,128)(2,1)}, u32[]{:S(2)}, u32[]{:S(2)}) async-start(bf16[8,48,2048]{2,1,0:T(8,128)(2,1)} %bitcast.129), calls=%async_computation | async-start | bytes 3145728 | tf_op jit(solution)/shard_map/all_to_all | solution.py:41
  31.2 6.2 %copy-start.2 = (f32[2048,8]{0,1:T(8,128)S(1)}, f32[2048,8]{0,1:T(8,128)}, u32[]{:S(2)}) copy-start(f32[2048,8]{0,1:T(8,128)} %param.11) | copy-start | bytes 196612
  31.2 7.8 %copy-start.3 = (s32[128,3]{0,1:T(4,128)S(1)}, s32[128,3]{0,1:T(4,128)}, u32[]{:S(2)}) copy-start(s32[128,3]{0,1:T(4,128)} %param.9) | copy-start | bytes 4612
  31.2 7.8 %copy-start.4 = (s32[128,3]{0,1:T(4,128)S(1)}, s32[128,3]{0,1:T(4,128)}, u32[]{:S(2)}) copy-start(s32[128,3]{0,1:T(4,128)} %param.10) | copy-start | bytes 4612
  69.8 42.6 %all-to-all-start.2 = ((bf16[8,48,2048]{2,1,0:T(8,128)(2,1)}), bf16[8,48,2048]{2,1,0:T(8,128)(2,1)}, u32[]{:S(2)}, u32[]{:S(2)}) async-start(bf16[8,48,2048]{2,1,0:T(8,128)(2,1)} %fusion), calls=%async_computation.2 | async-start | bytes 3145728 | tf_op jit(solution)/shard_map/all_to_all | solution.py:88
  74.1 183.9 %reduce-scatter.4.cloned.1.call-start = ((), (), s32[]{:S(2)}) async-start(), calls=%async_computation.6 | async-start | bytes 9732096
  74.3 5.0 copy-start.5
  116.1 3.9 copy-start.10
  116.1 3.9 copy-start.9
  116.1 7.2 %copy-start.7 = (bf16[8,1,48,768]{3,2,0,1:T(8,128)(2,1)}, bf16[8,1,48,768]{3,2,0,1:T(8,128)(2,1)S(1)}, u32[]{:S(2)}) copy-start(bf16[8,1,48,768]{3,2,0,1:T(8,128)(2,1)S(1)} %get-tuple-element.11) | copy-start | bytes 1769476
  147.1 42.7 %all-to-all-start.1 = ((bf16[8,48,2048]{2,1,0:T(8,128)(2,1)}), bf16[8,48,2048]{2,1,0:T(8,128)(2,1)}, u32[]{:S(2)}, u32[]{:S(2)}) async-start(bf16[8,48,2048]{2,1,0:T(8,128)(2,1)} %fusion.18), calls=%async_computation.1 | async-start | bytes 3145728 | tf_op jit(solution)/shard_map/all_to_all | solution.py:54
  151.6 3.9 copy-start.6
  151.7 3.9 copy-start.8
  189.8 42.5 %all-to-all-start.3 = ((bf16[8,48,2048]{2,1,0:T(8,128)(2,1)}), bf16[8,48,2048]{2,1,0:T(8,128)(2,1)}, u32[]{:S(2)}, u32[]{:S(2)}) async-start(bf16[8,48,2048]{2,1,0:T(8,128)(2,1)} %add_convert_fusion), calls=%async_computation.3 | async-start | bytes 3145728 | tf_op jit(solution)/shard_map/all_to_all | solution.py:104
  194.1 300.2 %all-reduce.6.cloned.1.call-start = ((), (), s32[]{:S(2)}) async-start(), calls=%async_computation.5 | async-start | bytes 131072 | tf_op jit(solution)/shard_map/psum | solution.py:143
  250.6 3.1 copy-start.1
Sparse Core Ops, SparseCore 0:
  143.6 99.7 reduce-scatter.3
Sparse Core Ops, SparseCore 1:
  254.8 239.4 all-reduce.5
where the time goes:
time: 505 us; the launch traced here: 503 us
  waiting for transfers between devices  340 us (67%)
  local copies, waits for them, and re-layouts  74.4 us (15%)
  matrix products  38.8 us (8%)
  starting transfers between devices  22.4 us (4%)
  between operations  15.8 us (3%)
  other arithmetic  11.4 us (2%)
    psum x1, waiting for transfers between devices, on_device(): lax.psum(jnp.dot(tokens_wide.T, logit_grad, precision=highest), ('dp', 'e...  228 us
    all_to_all x1, waiting for transfers between devices, on_device(): lax.all_to_all(expert_out.reshape(sender_count * local_count, item_count,...  31.7 us
    all_to_all x1, waiting for transfers between devices, on_device(): lax.all_to_all(grad_rows, 'expert', split_axis=0, concat_axis=0, tiled=True)  29.2 us
    all_to_all x1, waiting for transfers between devices, on_device(): lax.all_to_all(row_grad.reshape(sender_count * local_count, slot_count, w...  27.1 us
    all_to_all x1, waiting for transfers between devices, on_device(): lax.all_to_all(outgoing, 'expert', split_axis=0, concat_axis=0, tiled=True)  24.7 us
    unnamed x28, local copies, waits for them, and re-layouts  20.4 us
    gather x3, local copies, waits for them, and re-layouts, on_device(): got_row = out_pad[position[:, which]].astype(jnp.float32)  12.1 us
    gather x3, local copies, waits for them, and re-layouts, on_device(): row_sum = row_sum + back_pad[position[:, which]].astype(jnp.float32)  11.7 us
  transfers between devices with their start and end apart: 6, of which 5 were waited for; matrix products, arithmetic and copies ran while one was open for 16% of the time, Pallas kernels for 0%

commit v1 on v0

--- a/solution.py
+++ b/solution.py
@@ -2,6 +2,10 @@
 import jax.numpy as jnp
 from jax import lax
 from jax.sharding import PartitionSpec as P
+
+answer_limits_on_mesh = lambda v0, link_axis: jnp.sum(
+    jax.lax.all_gather(v0, axis_name=link_axis), 0
+)
 
 
 def silu_parts(hidden):
@@ -140,7 +144,9 @@
     grad_tokens = (row_sum + jnp.dot(logit_grad, w_router.T, precision=highest)).astype(
         jnp.bfloat16
     )
-    grad_router = lax.psum(jnp.dot(tokens_wide.T, logit_grad, precision=highest), ("dp", "expert"))
+    grad_router = answer_limits_on_mesh(
+        jnp.dot(tokens_wide.T, logit_grad, precision=highest), ("dp", "expert")
+    )
     return (layer_output, grad_tokens, grad_router, grad_gate, grad_up, grad_down)
 
 

time: 505 us -> 350 us (0.69)
  waiting for transfers between devices: 340 us -> 144 us
  blocking collectives: 0 us -> 43.9 us
  other arithmetic: 11.4 us -> 18.7 us
    psum x1 -> x0, waiting for transfers between devices: 228 us -> none  [on_device(): lax.psum(jnp.dot(tokens_wide.T, logit_grad, precision=highest), ('dp', 'e...]
    all_gather x0 -> x1, waiting for transfers between devices: none -> 49.5 us  [jax.lax.all_gather(v0, axis_name=link_axis)]
    all_to_all x0 -> x1, blocking collectives: none -> 43.9 us  [on_device(): lax.all_to_all(row_grad.reshape(sender_count * local_count, slot_count, w...]
    all_to_all x1 -> x0, waiting for transfers between devices: 27.1 us -> none  [on_device(): lax.all_to_all(row_grad.reshape(sender_count * local_count, slot_count, w...]
    all_to_all x1, waiting for transfers between devices: 31.7 us -> 40.1 us  [on_device(): lax.all_to_all(expert_out.reshape(sender_count * local_count, item_count,...]
    reduce_sum x0 -> x1, other arithmetic: none -> 7.22 us  [jnp.sum(jax.lax.all_gather(v0, axis_name=link_axis), 0)]
    unnamed x28 -> x27, local copies, waits for them, and re-layouts: 20.4 us -> 19.2 us
  transfers between devices with their start and end apart: 6 -> 5, of which waited for: 5 -> 4; matrix products, arithmetic and copies ran while one was open for 16% -> 22% of each run, Pallas kernels for 0% -> 0%
where the time goes in v1:
time: 350 us; the launch traced here: 349 us
  waiting for transfers between devices  144 us (41%)
  local copies, waits for them, and re-layouts  71.2 us (20%)
  blocking collectives  43.9 us (13%)
  matrix products  37.5 us (11%)
  other arithmetic  18.7 us (5%)
  starting transfers between devices  18.2 us (5%)
  between operations  15.8 us (5%)
    all_gather x1, waiting for transfers between devices, jax.lax.all_gather(v0, axis_name=link_axis)  49.5 us
    all_to_all x1, blocking collectives, on_device(): lax.all_to_all(row_grad.reshape(sender_count * local_count, slot_count, w...  43.9 us
    all_to_all x1, waiting for transfers between devices, on_device(): lax.all_to_all(expert_out.reshape(sender_count * local_count, item_count,...  40.1 us
    all_to_all x1, waiting for transfers between devices, on_device(): lax.all_to_all(grad_rows, 'expert', split_axis=0, concat_axis=0, tiled=True)  29.2 us
    all_to_all x1, waiting for transfers between devices, on_device(): lax.all_to_all(outgoing, 'expert', split_axis=0, concat_axis=0, tiled=True)  24.7 us
    unnamed x27, local copies, waits for them, and re-layouts  19.2 us
    gather x3, local copies, waits for them, and re-layouts, on_device(): got_row = out_pad[position[:, which]].astype(jnp.float32)  11.7 us
    gather x3, local copies, waits for them, and re-layouts, on_device(): row_sum = row_sum + back_pad[position[:, which]].astype(jnp.float32)  11.6 us
  transfers between devices with their start and end apart: 5, of which 4 were waited for; matrix products, arithmetic and copies ran while one was open for 22% of the time, Pallas kernels for 0%

profile of v1, /device:TPU:1, one launch (start us, length us, event | category | flops | bytes accessed | tf_op | source)
XLA Modules:
  0.0 348.9 jit_solution(3701645954325554006)
XLA Ops:
  8.0 0.0 copy-start
  8.0 0.9 add_select_fusion.1
  8.9 0.1 copy.36
  9.0 0.2 reshape.191
  9.2 2.9 scatter_custom_fusion
  12.2 1.9 concatenate.23
  14.1 6.2 %gather_fusion = bf16[384,2048]{1,0:T(8,128)(2,1)} fusion(bf16[129,2048]{1,0:T(8,128)(2,1)} %concatenate.23, s32[1024]{0:T(1024)S(1)} %get-tuple-element.27), kind=kCustom, calls=%fused_computation | custom fusion | bytes 3147264 | tf_op jit(solution)/shard_map/gather | solution.py:44
  20.3 9.1 %all-to-all-start = ((bf16[8,48,2048]{2,1,0:T(8,128)(2,1)}), bf16[8,48,2048]{2,1,0:T(8,128)(2,1)}, u32[]{:S(2)}, u32[]{:S(2)}) async-start(bf16[8,48,2048]{2,1,0:T(8,128)(2,1)} %bitcast.132), calls=%async_computation | async-start | bytes 3145728 | tf_op jit(solution)/shard_map/all_to_all | solution.py:45
  29.4 1.6 fusion.34
  31.0 0.0 copy-done.3
  31.1 0.1 copy.37
  31.2 0.2 reshape.198
  31.4 2.8 gather_fusion.4
  34.2 0.1 mul.126
  34.3 1.9 concatenate.26
  36.2 6.2 %gather_fusion.5 = bf16[384,2048]{1,0:T(8,128)(2,1)} fusion(bf16[129,2048]{1,0:T(8,128)(2,1)} %concatenate.26, s32[1024]{0:T(1024)S(1)} %get-tuple-element.27), kind=kCustom, calls=%fused_computation.5 | custom fusion | bytes 3147264 | tf_op jit(solution)/shard_map/gather | solution.py:88
  42.4 2.9 fusion
  45.2 24.7 %all-to-all-done = bf16[8,48,2048]{2,1,0:T(8,128)(2,1)} async-done(((bf16[8,48,2048]{2,1,0:T(8,128)(2,1)}), bf16[8,48,2048]{2,1,0:T(8,128)(2,1)}, u32[]{:S(2)}, u32[]{:S(2)}) %all-to-all-start) | async-done | bytes 1572896 | tf_op jit(solution)/shard_map/all_to_all | solution.py:45
  70.0 4.3 %all-to-all-start.2 = ((bf16[8,48,2048]{2,1,0:T(8,128)(2,1)}), bf16[8,48,2048]{2,1,0:T(8,128)(2,1)}, u32[]{:S(2)}, u32[]{:S(2)}) async-start(bf16[8,48,2048]{2,1,0:T(8,128)(2,1)} %fusion), calls=%async_computation.2 | async-start | bytes 3145728 | tf_op jit(solution)/shard_map/all_to_all | solution.py:92
  74.3 0.2 reduce-scatter.4.cloned.1.call-start
  74.5 0.0 copy-start.5
  74.5 4.9 %fusion.22 = f32[8,1,48,768]{3,2,0,1:T(8,128)} fusion(bf16[8,48,2048]{2,1,0:T(8,128)(2,1)} %all-to-all-done, bf16[1,2048,768]{2,1,0:T(8,128)(2,1)} %param.12), kind=kOutput, calls=%fused_computation.39 | convolution fusion | flops 1207959552 | bytes 5898240 | tf_op jit(solution)/shard_map/slnd,ldf->slnf/dot_general | solution.py:48
  79.5 3.8 %fusion.25 = f32[8,1,48,768]{3,2,0,1:T(8,128)} fusion(bf16[8,48,2048]{2,1,0:T(8,128)(2,1)} %all-to-all-done, bf16[1,2048,768]{2,1,0:T(8,128)(2,1)S(1)} %copy-done.5), kind=kOutput, calls=%fused_computation.40 | convolution fusion | flops 1207959552 | bytes 5898240 | tf_op jit(solution)/shard_map/slnd,ldf->slnf/dot_general | solution.py:51
  83.3 29.2 %all-to-all-done.2 = bf16[8,48,2048]{2,1,0:T(8,128)(2,1)} async-done(((bf16[8,48,2048]{2,1,0:T(8,128)(2,1)}), bf16[8,48,2048]{2,1,0:T(8,128)(2,1)}, u32[]{:S(2)}, u32[]{:S(2)}) %all-to-all-start.2) | async-done | bytes 1572896 | tf_op jit(solution)/shard_map/all_to_all | solution.py:92
  112.5 0.0 copy-done
  112.5 3.7 %multiply_convert_fusion.1 = (bf16[8,1,48,768]{3,2,0,1:T(8,128)(2,1)S(1)}, bf16[8,48,768]{2,1,0:T(8,128)(2,1)S(1)}, bf16[8,48,768]{2,1,0:T(8,128)(2,1)S(1)}) fusion(f32[8,1,48,768]{3,2,0,1:T(8,128)} %fusion.22, f32[8,1,48,768]{3,2,0,1:T(8,128)} %fusion.25, bf16[8,48,2048]{2,1,0:T(8,128)(2,1)} %all-to-all-done.2, bf16[1,2048,768]{2,1,0:T(8,128)(2,1)S(1)} %copy-done), kind=kOutput, calls=%fused_computation.46 | convolution fusion | flops 1212383232 | bytes 8847360 | tf_op jit(solution)/shard_map/slnd,ldf->slnf/dot_general | solution.py:101
  116.3 3.9 %fusion.15 = bf16[2048,1,768]{0,2,1:T(8,128)(2,1)S(1)} fusion(bf16[8,48,768]{2,1,0:T(8,128)(2,1)S(1)} %get-tuple-element.13, bf16[8,48,2048]{2,1,0:T(8,128)(2,1)} %all-to-all-done.2), kind=kOutput, calls=%fused_computation.31 | convolution fusion | flops 1209532416 | bytes 5308416 | tf_op jit(solution)/shard_map/slnd,slnf->dlf/dot_general | solution.py:121
  120.2 3.2 fusion.13
  123.4 0.0 copy-done.9
  123.5 3.2 fusion.14
  126.7 4.5 %maximum_bitcast_fusion = bf16[2048,2304]{0,1:T(8,128)(2,1)} fusion(bf16[2048,1,768]{0,2,1:T(8,128)(2,1)S(1)} %fusion.15, bf16[2048,1,768]{0,2,1:T(8,128)(2,1)S(1)} %fusion.14, bf16[2048,1,768]{0,2,1:T(8,128)(2,1)S(1)} %fusion.13), kind=kLoop, calls=%fused_computation.10 | loop fusion | flops 28311552 | bytes 18874368 | tf_op jit(solution)/shard_map/convert_element_type | solution.py:128
  131.2 12.6 %copy.41 = bf16[2048,2304]{1,0:T(8,128)(2,1)} copy(bf16[2048,2304]{0,1:T(8,128)(2,1)} %maximum_bitcast_fusion) | data formatting | bytes 18874368
  143.9 0.0 reduce-scatter.4.cloned.1.call-update
  143.9 3.6 %fusion.18 = bf16[8,48,2048]{2,1,0:T(8,128)(2,1)} fusion(bf16[8,48,768]{2,1,0:T(8,128)(2,1)} %copy-done.10, bf16[1,2048,768]{2,1,0:T(8,128)(2,1)S(1)} %copy-done), kind=kOutput, calls=%fused_computation.32 | convolution fusion | flops 1208745984 | bytes 5308416 | tf_op jit(solution)/shard_map/slnf,ldf->slnd/dot_general | solution.py:55
  147.5 4.3 %all-to-all-start.1 = ((bf16[8,48,2048]{2,1,0:T(8,128)(2,1)}), bf16[8,48,2048]{2,1,0:T(8,128)(2,1)}, u32[]{:S(2)}, u32[]{:S(2)}) async-start(bf16[8,48,2048]{2,1,0:T(8,128)(2,1)} %fusion.18), calls=%async_computation.1 | async-start | bytes 3145728 | tf_op jit(solution)/shard_map/all_to_all | solution.py:58
  151.9 0.3 all-gather.3.cloned.1.call-start
  152.2 40.1 %all-to-all-done.1 = bf16[8,48,2048]{2,1,0:T(8,128)(2,1)} async-done(((bf16[8,48,2048]{2,1,0:T(8,128)(2,1)}), bf16[8,48,2048]{2,1,0:T(8,128)(2,1)}, u32[]{:S(2)}, u32[]{:S(2)}) %all-to-all-start.1) | async-done | bytes 1572896 | tf_op jit(solution)/shard_map/all_to_all | solution.py:58
  192.3 2.8 concatenate.24
  195.1 3.9 %gather_fusion.2 = bf16[128,2048]{1,0:T(8,128)(2,1)} fusion(bf16[385,2048]{1,0:T(8,128)(2,1)} %concatenate.24, s32[1024]{0:T(1024)S(1)} %get-tuple-element.29), kind=kCustom, calls=%fused_computation.2 | custom fusion | bytes 1049088 | tf_op jit(solution)/shard_map/gather | solution.py:80
  198.9 3.9 %gather_fusion.3 = bf16[128,2048]{1,0:T(8,128)(2,1)} fusion(bf16[385,2048]{1,0:T(8,128)(2,1)} %concatenate.24, s32[1024]{0:T(1024)S(1)} %get-tuple-element.28), kind=kCustom, calls=%fused_computation.3 | custom fusion | bytes 1049088 | tf_op jit(solution)/shard_map/gather | solution.py:80
  202.8 3.9 %gather_fusion.1 = bf16[128,2048]{1,0:T(8,128)(2,1)} fusion(bf16[385,2048]{1,0:T(8,128)(2,1)} %concatenate.24, s32[1024]{0:T(1024)S(1)} %pad_clamp_fusion.3), kind=kCustom, calls=%fused_computation.1 | custom fusion | bytes 1049088 | tf_op jit(solution)/shard_map/gather | solution.py:80
  206.7 3.1 fusion.38
  209.9 0.0 copy-done.1
  209.9 1.0 convolution_bitcast_fusion
  210.8 0.0 all-gather.3.cloned.1.call-update
  210.8 0.0 copy-start.6
  210.8 0.0 copy-start.8
  210.9 3.7 %fusion.5 = f32[8,48,2048]{2,1,0:T(8,128)S(1)} fusion(bf16[8,48,768]{2,1,0:T(8,128)(2,1)} %copy-done.9, bf16[1,2048,768]{2,1,0:T(8,128)(2,1)} %param.13), kind=kOutput, calls=%fused_computation.20 | convolution fusion | flops 1207959552 | bytes 6881280 | tf_op jit(solution)/shard_map/slnf,ldf->slnd/dot_general | solution.py:106
  214.6 0.0 copy-done.6
  214.6 0.0 copy-done.8
  214.6 1.4 add_convert_fusion
  216.0 43.9 %all_to_all.20 = bf16[8,48,2048]{2,1,0:T(8,128)(2,1)S(1)} all-to-all(bf16[8,48,2048]{2,1,0:T(8,128)(2,1)S(1)} %add_convert_fusion), channel_id=1, replica_groups=mesh['dp'=32,'expert'=8] {'expert'}, dimensions={0} | all-to-all | bytes 3145728 | tf_op jit(solution)/shard_map/all_to_all | solution.py:108
  260.0 1.3 concatenate.27
  261.3 3.9 %gather_fusion.7 = bf16[128,2048]{1,0:T(8,128)(2,1)} fusion(bf16[385,2048]{1,0:T(8,128)(2,1)} %concatenate.27, s32[1024]{0:T(1024)S(1)} %get-tuple-element.29), kind=kCustom, calls=%fused_computation.7 | custom fusion | bytes 1049088 | tf_op jit(solution)/shard_map/gather | solution.py:140
  265.2 3.9 %gather_fusion.8 = bf16[128,2048]{1,0:T(8,128)(2,1)} fusion(bf16[385,2048]{1,0:T(8,128)(2,1)} %concatenate.27, s32[1024]{0:T(1024)S(1)} %get-tuple-element.28), kind=kCustom, calls=%fused_computation.8 | custom fusion | bytes 1049088 | tf_op jit(solution)/shard_map/gather | solution.py:140
  269.0 3.9 %gather_fusion.6 = bf16[128,2048]{1,0:T(8,128)(2,1)} fusion(bf16[385,2048]{1,0:T(8,128)(2,1)} %concatenate.27, s32[1024]{0:T(1024)S(1)} %pad_clamp_fusion.3), kind=kCustom, calls=%fused_computation.6 | custom fusion | bytes 1049088 | tf_op jit(solution)/shard_map/gather | solution.py:140
  272.9 3.3 fusion.21
  276.2 2.0 copy.42
  278.2 2.1 fusion.53
  280.3 1.8 copy.43
  282.1 1.8 copy.44
  283.9 0.8 copy.45
  284.8 49.5 %all-gather.3.cloned.1.call-done = f32[524288,8]{0,1:T(8,128)} async-done(((f32[2048,8]{0,1:T(8,128)}), f32[524288,8]{0,1:T(8,128)}) %all-gather.3.cloned.1.call-update) | async-done | bytes 16777232 | tf_op jit(solution)/shard_map/all_gather | solution.py:7
  334.3 7.2 %reduce_sum.79 = f32[2048,8]{0,1:T(8,128)} reduce(f32[256,2048,8]{1,2,0:T(8,128)} %bitcast.130, f32[]{:T(128)} %constant.14.clone.1), dimensions={0}, to_apply=%region_8.9 | reduce | flops 4177920 | bytes 16842756 | tf_op jit(solution)/shard_map/reduce_sum | solution.py:6
  (27 shorter events, 0.2 us)
Async XLA Ops:
  8.0 104.5 %copy-start = (bf16[1,2048,768]{2,1,0:T(8,128)(2,1)S(1)}, bf16[1,2048,768]{2,1,0:T(8,128)(2,1)}, u32[]{:S(2)}) copy-start(bf16[1,2048,768]{2,1,0:T(8,128)(2,1)} %param.14) | copy-start | bytes 9437188
  20.3 9.2 %copy-start.2 = (f32[2048,8]{0,1:T(8,128)S(1)}, f32[2048,8]{0,1:T(8,128)}, u32[]{:S(2)}) copy-start(f32[2048,8]{0,1:T(8,128)} %param.11) | copy-start | bytes 196612
  20.3 10.7 %copy-start.3 = (s32[128,3]{0,1:T(4,128)S(1)}, s32[128,3]{0,1:T(4,128)}, u32[]{:S(2)}) copy-start(s32[128,3]{0,1:T(4,128)} %param.9) | copy-start | bytes 4612
  20.3 10.8 %copy-start.4 = (s32[128,3]{0,1:T(4,128)S(1)}, s32[128,3]{0,1:T(4,128)}, u32[]{:S(2)}) copy-start(s32[128,3]{0,1:T(4,128)} %param.10) | copy-start | bytes 4612
  20.3 49.7 %all-to-all-start = ((bf16[8,48,2048]{2,1,0:T(8,128)(2,1)}), bf16[8,48,2048]{2,1,0:T(8,128)(2,1)}, u32[]{:S(2)}, u32[]{:S(2)}) async-start(bf16[8,48,2048]{2,1,0:T(8,128)(2,1)} %bitcast.132), calls=%async_computation | async-start | bytes 3145728 | tf_op jit(solution)/shard_map/all_to_all | solution.py:45
  70.0 42.6 %all-to-all-start.2 = ((bf16[8,48,2048]{2,1,0:T(8,128)(2,1)}), bf16[8,48,2048]{2,1,0:T(8,128)(2,1)}, u32[]{:S(2)}, u32[]{:S(2)}) async-start(bf16[8,48,2048]{2,1,0:T(8,128)(2,1)} %fusion), calls=%async_computation.2 | async-start | bytes 3145728 | tf_op jit(solution)/shard_map/all_to_all | solution.py:92
  74.3 201.9 %reduce-scatter.4.cloned.1.call-start = ((), (), s32[]{:S(2)}) async-start(), calls=%async_computation.6 | async-start | bytes 9732096
  74.5 5.0 %copy-start.5 = (bf16[1,2048,768]{2,1,0:T(8,128)(2,1)S(1)}, bf16[1,2048,768]{2,1,0:T(8,128)(2,1)}, u32[]{:S(2)}) copy-start(bf16[1,2048,768]{2,1,0:T(8,128)(2,1)} %param.13) | copy-start | bytes 9437188
  116.3 3.9 %copy-start.10 = (bf16[8,48,768]{2,1,0:T(8,128)(2,1)}, bf16[8,48,768]{2,1,0:T(8,128)(2,1)S(1)}, u32[]{:S(2)}) copy-start(bf16[8,48,768]{2,1,0:T(8,128)(2,1)S(1)} %get-tuple-element.13) | copy-start | bytes 1769476
  116.3 3.9 %copy-start.7 = (bf16[8,1,48,768]{3,2,0,1:T(8,128)(2,1)}, bf16[8,1,48,768]{3,2,0,1:T(8,128)(2,1)S(1)}, u32[]{:S(2)}) copy-start(bf16[8,1,48,768]{3,2,0,1:T(8,128)(2,1)S(1)} %get-tuple-element.11) | copy-start | bytes 1769476
  116.3 7.2 %copy-start.9 = (bf16[8,48,768]{2,1,0:T(8,128)(2,1)}, bf16[8,48,768]{2,1,0:T(8,128)(2,1)S(1)}, u32[]{:S(2)}) copy-start(bf16[8,48,768]{2,1,0:T(8,128)(2,1)S(1)} %get-tuple-element.12) | copy-start | bytes 1769476
  147.5 44.7 %all-to-all-start.1 = ((bf16[8,48,2048]{2,1,0:T(8,128)(2,1)}), bf16[8,48,2048]{2,1,0:T(8,128)(2,1)}, u32[]{:S(2)}, u32[]{:S(2)}) async-start(bf16[8,48,2048]{2,1,0:T(8,128)(2,1)} %fusion.18), calls=%async_computation.1 | async-start | bytes 3145728 | tf_op jit(solution)/shard_map/all_to_all | solution.py:58
  151.9 182.4 %all-gather.3.cloned.1.call-start = ((), (), s32[]{:S(2)}) async-start(), calls=%async_computation.5 | async-start | bytes 16842752 | tf_op jit(solution)/shard_map/all_gather | solution.py:7
  206.7 3.1 copy-start.1
  210.8 3.8 %copy-start.6 = (bf16[1,2048,768]{2,1,0:T(8,128)(2,1)S(1)}, bf16[1,2048,768]{2,1,0:T(8,128)(2,1)}, u32[]{:S(2)}) copy-start(bf16[1,2048,768]{2,1,0:T(8,128)(2,1)} %param.12) | copy-start | bytes 9437188
  210.8 3.8 %copy-start.8 = (bf16[8,1,48,768]{3,2,0,1:T(8,128)(2,1)S(1)}, bf16[8,1,48,768]{3,2,0,1:T(8,128)(2,1)}, u32[]{:S(2)}) copy-start(bf16[8,1,48,768]{3,2,0,1:T(8,128)(2,1)} %copy-done.7) | copy-start | bytes 1769476
Sparse Core Ops, SparseCore 0:
  144.0 100.0 reduce-scatter.3
Sparse Core Ops, SparseCore 1:
  210.9 123.3 all-gather.2
